TPU v7x, 32 devices: a whole 2x2x4 slice. The times are simulated.
32 devices in a mesh: dp: 8 (over z, core), shard: 4 (over y, x).
Axes of the slice: x: 2, y: 2, z: 4, core: 2. Of those that a mesh axis runs over, the one named last changes fastest.
Arguments:
- grad_partials: bfloat16 [8, 32, 256, 256], P('dp', 'shard'), may hold values from -8 to 8
- owners: int32 [32, 1], P('shard'), may hold values from 0 to 7; in each aligned block of 8 rows (0 to 7, 8 to 15, ...) at most 2 rows name the same one
- weight_blocks: int32 [9], replicated, may hold values from 1 to 8, 32 in all
- stats_left: float32 [8, 4, 2, 256, 256], P('dp', 'shard'), may hold values from -6 to 6
- stats_right: float32 [8, 4, 2, 256, 256], P('dp', 'shard'), may hold values from -6 to 6
- root_left: bfloat16 [8, 4, 2, 256, 256], P('dp', 'shard'), may hold values from -0.375 to 0.375
- root_right: bfloat16 [8, 4, 2, 256, 256], P('dp', 'shard'), may hold values from -0.375 to 0.375
- second_moment: float32 [8, 4, 2, 256, 256], P('dp', 'shard'), may hold values from 0.0015 to 0.6
- master: float32 [8, 4, 2, 256, 256], P('dp', 'shard'), may hold values from -6 to 6
Outputs:
- new_left: float32 [8, 4, 2, 256, 256], P('dp', 'shard')
- new_right: float32 [8, 4, 2, 256, 256], P('dp', 'shard')
- new_moment: float32 [8, 4, 2, 256, 256], P('dp', 'shard')
- new_master: float32 [8, 4, 2, 256, 256], P('dp', 'shard')
- regathered: bfloat16 [32, 256, 256], P('shard')
Inputs may be any that keep to these rules, and one draw needn't show every extreme that they name: `owners`: in each aligned block of 8 rows (one column) no dp index is named more than 2 times; some column names one exactly 2 times. `weight_blocks`: sums to 32; the largest is 8.
All inputs are finite; a program needn't handle non-finite values.
Results may differ from a plain program's by a relative error of at most 0.0047.
Values may be sent and summed in bfloat16 or wider, within the bound.
No kernel may reach another device: no remote copies, remote signals or barrier semaphores. Data moves between devices by JAX's collectives and lax.ppermute only.
A program may use at most 128 MiB of HBM per device.

v0:
```python
import jax
import jax.numpy as jnp
from jax import lax
from jax.sharding import PartitionSpec as P

BETA = 0.95
RATE = 0.3
ADAM_EPS = 1e-08
NORM_EPS = 1e-06


def butterfly_sum(x, axis):
    size = lax.axis_size(axis)
    if size & size - 1:
        return lax.psum(x, axis)
    step = 1
    while step < size:
        x = x + lax.ppermute(x, axis, [(i, i ^ step) for i in range(size)])
        step *= 2
    return x


def local(
    grad_partials,
    owners,
    weight_blocks,
    stats_left,
    stats_right,
    root_left,
    root_right,
    second_moment,
    master,
):
    replica = lax.axis_index("dp")
    column = lax.axis_index("shard")
    replicas = lax.axis_size("dp")
    local_grads = grad_partials[0]
    column_blocks = local_grads.shape[0]
    slot_count = stats_left.shape[2]
    owner_of = owners[:, 0]
    onehot = (owner_of[:, None] == jnp.arange(replicas, dtype=jnp.int32)[None, :]).astype(jnp.int32)
    slot_rank = jnp.sum((jnp.cumsum(onehot, axis=0) - onehot) * onehot, axis=1)
    matches = (owner_of[None, None, :] == jnp.arange(replicas, dtype=jnp.int32)[:, None, None]) & (
        slot_rank[None, None, :] == jnp.arange(slot_count, dtype=jnp.int32)[None, :, None]
    )
    slot_table = jnp.sum(
        matches.astype(jnp.int32) * jnp.arange(column_blocks, dtype=jnp.int32)[None, None, :],
        axis=2,
    )
    slot_live = jnp.any(matches, axis=2)
    my_table = lax.dynamic_index_in_dim(slot_table, replica, 0, keepdims=False)
    my_live = lax.dynamic_index_in_dim(slot_live, replica, 0, keepdims=False)
    live_float = my_live.astype(jnp.float32)[:, None, None]
    summed = lax.psum(local_grads.astype(jnp.float32), "dp")
    owned_grad = jnp.take(summed, my_table, axis=0) * live_float
    left = stats_left[0, 0]
    right = stats_right[0, 0]
    moment = second_moment[0, 0]
    weights = master[0, 0]
    global_block = column * column_blocks + my_table
    ends = jnp.cumsum(weight_blocks)
    weight_id = jnp.sum((global_block[:, None] >= ends[None, :]).astype(jnp.int32), axis=1)
    member = (
        weight_id[:, None] == jnp.arange(weight_blocks.shape[0], dtype=jnp.int32)[None, :]
    ).astype(jnp.float32) * my_live.astype(jnp.float32)[:, None]
    vnew = BETA * moment + (1.0 - BETA) * owned_grad * owned_grad
    adam = owned_grad / (jnp.sqrt(vnew) + ADAM_EPS)
    adam_terms = jnp.sum(member * jnp.sum(adam * adam, axis=(1, 2))[:, None], axis=0)
    highest = lax.Precision.HIGHEST
    lnew = BETA * left + (1.0 - BETA) * jnp.einsum(
        "sij,skj->sik", owned_grad, owned_grad, precision=highest
    )
    rnew = BETA * right + (1.0 - BETA) * jnp.einsum(
        "sji,sjk->sik", owned_grad, owned_grad, precision=highest
    )
    grad_half = owned_grad.astype(jnp.bfloat16)
    inner = jnp.einsum(
        "sij,sjk->sik", root_left[0, 0], grad_half, preferred_element_type=jnp.float32
    ).astype(jnp.bfloat16)
    precond = jnp.einsum(
        "sij,sjk->sik", inner, root_right[0, 0], preferred_element_type=jnp.float32
    )
    prec_terms = jnp.sum(member * jnp.sum(precond * precond, axis=(1, 2))[:, None], axis=0)
    norms = butterfly_sum(butterfly_sum(jnp.stack([adam_terms, prec_terms]), "dp"), "shard")
    norm_adam = norms[0]
    norm_prec = norms[1]
    scales = jnp.sqrt(norm_adam / (norm_prec + NORM_EPS))
    slot_scale = jnp.sum(member * scales[None, :], axis=1)
    wnew = weights - RATE * slot_scale[:, None, None] * precond
    live_mask = my_live[:, None, None]
    out_left = jnp.where(live_mask, lnew, left)
    out_right = jnp.where(live_mask, rnew, right)
    out_moment = jnp.where(live_mask, vnew, moment)
    out_master = jnp.where(live_mask, wnew, weights)
    gathered = lax.all_gather(out_master.astype(jnp.bfloat16), "dp", axis=0, tiled=True)
    regathered = jnp.take(gathered, owner_of * slot_count + slot_rank, axis=0)
    return (
        out_left[None, None],
        out_right[None, None],
        out_moment[None, None],
        out_master[None, None],
        regathered,
    )


def solution(mesh):
    in_specs = (
        P("dp", "shard", None, None),
        P("shard", None),
        P(),
        P("dp", "shard", None, None, None),
        P("dp", "shard", None, None, None),
        P("dp", "shard", None, None, None),
        P("dp", "shard", None, None, None),
        P("dp", "shard", None, None, None),
        P("dp", "shard", None, None, None),
    )
    out_specs = (
        P("dp", "shard", None, None, None),
        P("dp", "shard", None, None, None),
        P("dp", "shard", None, None, None),
        P("dp", "shard", None, None, None),
        P("shard", None, None),
    )
    return jax.shard_map(local, mesh=mesh, in_specs=in_specs, out_specs=out_specs, check_vma=False)
```

profile of v0, /device:TPU:0, one launch (start us, length us, event | category | flops | bytes accessed | tf_op | source)
XLA Modules:
  0.0 138.4 jit_solution(13024483994053994536)
XLA Ops:
  7.2 2.7 %bitcast_convert_fusion = f32[8,256,256]{2,1,0:T(8,128)} fusion(bf16[1,8,256,256]{3,2,1,0:T(8,128)(2,1)} %param.9), kind=kLoop, calls=%fused_computation.12 | loop fusion | flops 524288 | bytes 3145728 | tf_op jit(solution)/shard_map/convert_element_type | solution.py:54
  10.1 0.1 iota_compare_fusion.1
  10.2 0.2 select_reduce_fusion
  10.4 0.1 and_reduce_fusion
  10.5 0.2 dynamic-slice_reduce_fusion
  10.7 0.1 fusion.34
  10.9 0.2 dynamic-slice_reduce_fusion.1
  11.1 0.2 reduce-window.8
  11.3 0.2 fusion.36
  11.5 66.6 %all-reduce.2.cloned.1.call-done = f32[8,256,256]{2,1,0:T(8,128)} async-done(((f32[8,256,256]{2,1,0:T(8,128)}), f32[8,256,256]{2,1,0:T(8,128)}) %all-reduce.2.cloned.1.call-update) | async-done | bytes 2097168 | tf_op jit(solution)/shard_map/psum | solution.py:54
  78.1 2.2 %gather_fusion = f32[2,256,256]{2,1,0:T(8,128)S(1)} fusion(f32[8,256,256]{2,1,0:T(8,128)} %all-reduce.2.cloned.1.call-done, s32[1024]{0:T(1024)S(1)} %pad_clamp_fusion.1), kind=kCustom, calls=%fused_computation | custom fusion | bytes 1048584 | tf_op jit(solution)/shard_map/jit(_take)/gather | solution.py:55
  80.2 0.5 fusion.15
  80.7 0.7 multiply_reduce_fusion
  81.4 0.1 multiply_reduce_fusion.3
  81.5 0.1 collective-permute-start
  81.6 1.1 collective-permute-done
  82.7 1.2 collective-permute-start.1
  84.0 2.4 %collective-permute-done.1 = f32[2,9]{1,0:T(2,128)S(1)} collective-permute-done((f32[2,9]{1,0:T(2,128)S(1)}, f32[2,9]{1,0:T(2,128)S(1)}, u32[]{:S(2)}, u32[]{:S(2)}) %collective-permute-start.1) | collective-permute-done | bytes 104 | tf_op jit(solution)/shard_map/ppermute | solution.py:18
  86.4 1.1 collective-permute-start.2
  87.5 3.4 %collective-permute-done.2 = f32[2,9]{1,0:T(2,128)S(1)} collective-permute-done((f32[2,9]{1,0:T(2,128)S(1)}, f32[2,9]{1,0:T(2,128)S(1)}, u32[]{:S(2)}, u32[]{:S(2)}) %collective-permute-start.2) | collective-permute-done | bytes 104 | tf_op jit(solution)/shard_map/ppermute | solution.py:18
  90.9 1.5 %collective-permute-start.3 = (f32[2,9]{1,0:T(2,128)S(1)}, f32[2,9]{1,0:T(2,128)S(1)}, u32[]{:S(2)}, u32[]{:S(2)}) collective-permute-start(f32[2,9]{1,0:T(2,128)S(1)} %add.94), channel_id=1, source_target_pairs={{0,1},{1,0},{2,3},{3,2},{4,5},{5,4},{6,7},{7,6},{8,9},{9,8},{10,11... | collective-permute-start | bytes 224 | tf_op jit(solution)/shard_map/ppermute | solution.py:18
  92.4 2.1 %collective-permute-done.3 = f32[2,9]{1,0:T(2,128)S(1)} collective-permute-done((f32[2,9]{1,0:T(2,128)S(1)}, f32[2,9]{1,0:T(2,128)S(1)}, u32[]{:S(2)}, u32[]{:S(2)}) %collective-permute-start.3) | collective-permute-done | bytes 104 | tf_op jit(solution)/shard_map/ppermute | solution.py:18
  94.5 1.5 %collective-permute-start.4 = (f32[2,9]{1,0:T(2,128)S(1)}, f32[2,9]{1,0:T(2,128)S(1)}, u32[]{:S(2)}, u32[]{:S(2)}) collective-permute-start(f32[2,9]{1,0:T(2,128)S(1)} %add.95), channel_id=1, source_target_pairs={{0,2},{1,3},{2,0},{3,1},{4,6},{5,7},{6,4},{7,5},{8,10},{9,11},{10,... | collective-permute-start | bytes 224 | tf_op jit(solution)/shard_map/ppermute | solution.py:18
  96.0 2.1 %collective-permute-done.4 = f32[2,9]{1,0:T(2,128)S(1)} collective-permute-done((f32[2,9]{1,0:T(2,128)S(1)}, f32[2,9]{1,0:T(2,128)S(1)}, u32[]{:S(2)}, u32[]{:S(2)}) %collective-permute-start.4) | collective-permute-done | bytes 104 | tf_op jit(solution)/shard_map/ppermute | solution.py:18
  98.1 0.2 multiply_reduce_fusion.1
  98.3 1.0 fusion.43
  99.4 2.0 %fusion.2 = f32[1,1,2,256,256]{4,3,2,1,0:T(8,128)} fusion(f32[1,1,2,256,256]{4,3,2,1,0:T(8,128)S(1)} %copy-done.3, f32[2,256,256]{2,1,0:T(8,128)S(1)} %gather_fusion, f32[2]{0:T(128)S(1)} %convert_element_type.39, pred[2]{0:T(512)(128)(4,1)S(1)} %compare_and_fusion, pred[2]{0:T(512)(128)(4,1)S(1)} %dynamic-slice_reduce_fusion), kind=kOutput, calls=%fused_computation.5 | convolution fusion | flops 403439616 | bytes 1572876 | tf_op jit(solution)/shard_map/sji,sjk->sik/dot_general | solution.py:73
  101.3 1.7 %fusion.5 = f32[1,1,2,256,256]{4,3,2,1,0:T(8,128)} fusion(f32[1,1,2,256,256]{4,3,2,1,0:T(8,128)S(1)} %copy-done.4, f32[2,256,256]{2,1,0:T(8,128)S(1)} %gather_fusion, f32[2]{0:T(128)S(1)} %convert_element_type.39, pred[2]{0:T(512)(128)(4,1)S(1)} %compare_and_fusion, pred[2]{0:T(512)(128)(4,1)S(1)} %dynamic-slice_reduce_fusion), kind=kOutput, calls=%fused_computation.9 | convolution fusion | flops 403439616 | bytes 1572876 | tf_op jit(solution)/shard_map/sij,skj->sik/dot_general | solution.py:70
  103.0 1.0 fusion.8
  104.0 24.3 %all-gather.2.cloned.1.call-done = bf16[16,256,256]{2,1,0:T(8,128)(2,1)} async-done(((bf16[2,256,256]{2,1,0:T(8,128)(2,1)}), bf16[16,256,256]{2,1,0:T(8,128)(2,1)}) %all-gather.2.cloned.1.call-update) | async-done | bytes 2097168 | tf_op jit(solution)/shard_map/all_gather | solution.py:95
  128.2 2.2 %gather_fusion.1 = bf16[8,256,256]{2,1,0:T(8,128)(2,1)S(1)} fusion(bf16[16,256,256]{2,1,0:T(8,128)(2,1)} %all-gather.2.cloned.1.call-done, s32[1024]{0:T(1024)S(1)} %pad_clamp_fusion), kind=kCustom, calls=%fused_computation.1 | custom fusion | bytes 2097184 | tf_op jit(solution)/shard_map/jit(_take)/gather | solution.py:96
  130.5 1.1 broadcast_select_fusion
  (37 shorter events, 0.3 us)
Async XLA Ops:
  7.2 73.6 %copy-start = (bf16[1,1,2,256,256]{4,3,2,1,0:T(8,128)(2,1)S(1)}, bf16[1,1,2,256,256]{4,3,2,1,0:T(8,128)(2,1)}, u32[]{:S(2)}) copy-start(bf16[1,1,2,256,256]{4,3,2,1,0:T(8,128)(2,1)} %param.15) | copy-start | bytes 786436
  7.2 2.9 %copy-start.6 = (s32[8,1]{0,1:T(1,128)S(1)}, s32[8,1]{0,1:T(1,128)}, u32[]{:S(2)}) copy-start(s32[8,1]{0,1:T(1,128)} %param.10) | copy-start | bytes 100
  7.2 3.9 %copy-start.7 = (s32[9]{0:T(128)S(1)}, s32[9]{0:T(128)}, u32[]{:S(2)}) copy-start(s32[9]{0:T(128)} %param.11) | copy-start | bytes 112
  7.2 70.9 %all-reduce.2.cloned.1.call-start = ((), (), s32[]{:S(2)}) async-start(), calls=%async_computation | async-start | bytes 4194304 | tf_op jit(solution)/shard_map/psum | solution.py:54
  10.0 70.2 %copy-start.1 = (f32[1,1,2,256,256]{4,3,2,1,0:T(8,128)S(1)}, f32[1,1,2,256,256]{4,3,2,1,0:T(8,128)}, u32[]{:S(2)}) copy-start(f32[1,1,2,256,256]{4,3,2,1,0:T(8,128)} %param.16) | copy-start | bytes 1572868
  10.0 70.7 %copy-start.5 = (bf16[1,1,2,256,256]{4,3,2,1,0:T(8,128)(2,1)S(1)}, bf16[1,1,2,256,256]{4,3,2,1,0:T(8,128)(2,1)}, u32[]{:S(2)}) copy-start(bf16[1,1,2,256,256]{4,3,2,1,0:T(8,128)(2,1)} %param.14) | copy-start | bytes 786436
  10.0 88.3 %copy-start.2 = (f32[1,1,2,256,256]{4,3,2,1,0:T(8,128)S(1)}, f32[1,1,2,256,256]{4,3,2,1,0:T(8,128)}, u32[]{:S(2)}) copy-start(f32[1,1,2,256,256]{4,3,2,1,0:T(8,128)} %param.17) | copy-start | bytes 1572868
  10.0 118.2 %all-gather.2.cloned.1.call-start = ((), (), s32[]{:S(2)}) async-start(), calls=%async_computation.1 | async-start | bytes 2359296 | tf_op jit(solution)/shard_map/all_gather | solution.py:95
  80.7 18.6 %copy-start.3 = (f32[1,1,2,256,256]{4,3,2,1,0:T(8,128)S(1)}, f32[1,1,2,256,256]{4,3,2,1,0:T(8,128)}, u32[]{:S(2)}) copy-start(f32[1,1,2,256,256]{4,3,2,1,0:T(8,128)} %param.13) | copy-start | bytes 1572868
  81.4 19.9 %copy-start.4 = (f32[1,1,2,256,256]{4,3,2,1,0:T(8,128)S(1)}, f32[1,1,2,256,256]{4,3,2,1,0:T(8,128)}, u32[]{:S(2)}) copy-start(f32[1,1,2,256,256]{4,3,2,1,0:T(8,128)} %param.12) | copy-start | bytes 1572868
  81.5 1.2 collective-permute-start
  82.7 3.6 %collective-permute-start.1 = (f32[2,9]{1,0:T(2,128)S(1)}, f32[2,9]{1,0:T(2,128)S(1)}, u32[]{:S(2)}, u32[]{:S(2)}) collective-permute-start(f32[2,9]{1,0:T(2,128)S(1)} %fusion.42), channel_id=1, source_target_pairs={{0,8},{4,12},{8,0},{12,4},{16,24},{20,28},{24,16},{28,20},{1,9},{5... | collective-permute-start | bytes 224 | tf_op jit(solution)/shard_map/ppermute | solution.py:18
  86.4 4.5 %collective-permute-start.2 = (f32[2,9]{1,0:T(2,128)S(1)}, f32[2,9]{1,0:T(2,128)S(1)}, u32[]{:S(2)}, u32[]{:S(2)}) collective-permute-start(f32[2,9]{1,0:T(2,128)S(1)} %fusion.49), channel_id=1, source_target_pairs={{0,16},{4,20},{8,24},{12,28},{16,0},{20,4},{24,8},{28,12},{1,17},{... | collective-permute-start | bytes 224 | tf_op jit(solution)/shard_map/ppermute | solution.py:18
  90.9 3.6 %collective-permute-start.3 = (f32[2,9]{1,0:T(2,128)S(1)}, f32[2,9]{1,0:T(2,128)S(1)}, u32[]{:S(2)}, u32[]{:S(2)}) collective-permute-start(f32[2,9]{1,0:T(2,128)S(1)} %add.94), channel_id=1, source_target_pairs={{0,1},{1,0},{2,3},{3,2},{4,5},{5,4},{6,7},{7,6},{8,9},{9,8},{10,11... | collective-permute-start | bytes 224 | tf_op jit(solution)/shard_map/ppermute | solution.py:18
  94.5 3.6 %collective-permute-start.4 = (f32[2,9]{1,0:T(2,128)S(1)}, f32[2,9]{1,0:T(2,128)S(1)}, u32[]{:S(2)}, u32[]{:S(2)}) collective-permute-start(f32[2,9]{1,0:T(2,128)S(1)} %add.95), channel_id=1, source_target_pairs={{0,2},{1,3},{2,0},{3,1},{4,6},{5,7},{6,4},{7,5},{8,10},{9,11},{10,... | collective-permute-start | bytes 224 | tf_op jit(solution)/shard_map/ppermute | solution.py:18
Sparse Core Ops, SparseCore 0:
  10.4 67.6 all-reduce.1
  99.5 28.7 all-gather.1
where the time goes:
time: 139 us; the launch traced here: 138 us
  waiting for transfers between devices  102 us (73%)
  between operations  14.2 us (10%)
  other arithmetic  7.71 us (6%)
  starting transfers between devices  5.47 us (4%)
  local copies, waits for them, and re-layouts  4.78 us (3%)
  matrix products  4.3 us (3%)
    psum x1, waiting for transfers between devices, local(): summed = lax.psum(local_grads.astype(jnp.float32), 'dp')  66.6 us
    all_gather x1, waiting for transfers between devices, local(): lax.all_gather(out_master.astype(jnp.bfloat16), 'dp', axis=0, tiled=True)  24.3 us
    ppermute x5, waiting for transfers between devices, butterfly_sum(): x = x + lax.ppermute(x, axis, [(i, i ^ step) for i in range(size)])  11.1 us
    ppermute x5, starting transfers between devices, butterfly_sum(): x = x + lax.ppermute(x, axis, [(i, i ^ step) for i in range(size)])  5.39 us
  transfers between devices with their start and end apart: 7, of which 7 were waited for; matrix products, arithmetic and copies ran while one was open for 4% of the time, Pallas kernels for 0%

commit v1 on v0

--- a/solution.py
+++ b/solution.py
@@ -51,7 +51,7 @@
     my_table = lax.dynamic_index_in_dim(slot_table, replica, 0, keepdims=False)
     my_live = lax.dynamic_index_in_dim(slot_live, replica, 0, keepdims=False)
     live_float = my_live.astype(jnp.float32)[:, None, None]
-    summed = lax.psum(local_grads.astype(jnp.float32), "dp")
+    summed = jnp.sum(lax.all_gather(local_grads.astype(jnp.float32), "dp"), axis=0)
     owned_grad = jnp.take(summed, my_table, axis=0) * live_float
     left = stats_left[0, 0]
     right = stats_right[0, 0]

time: 139 us -> 230 us (1.65)
  waiting for transfers between devices: 102 us -> 188 us
  other arithmetic: 7.71 us -> 14.9 us
    all_gather x0 -> x1, waiting for transfers between devices: none -> 152 us  [local(): lax.all_gather(local_grads.astype(jnp.float32), 'dp')]
    psum x1 -> x0, waiting for transfers between devices: 66.6 us -> none  [local(): summed = lax.psum(local_grads.astype(jnp.float32), 'dp')]
    reduce_sum x0 -> x1, other arithmetic: none -> 7.15 us  [local(): jnp.sum(lax.all_gather(local_grads.astype(jnp.float32), 'dp'), axis=0)]
  transfers between devices with their start and end apart: 7 -> 7, of which waited for: 7 -> 7; matrix products, arithmetic and copies ran while one was open for 4% -> 3% of each run, Pallas kernels for 0% -> 0%
where the time goes in v1:
time: 230 us
  waiting for transfers between devices  188 us (82%)
  other arithmetic  14.9 us (6%)
  between operations  14.2 us (6%)
  matrix products  5.31 us (2%)
  starting transfers between devices  4.11 us (2%)
  local copies, waits for them, and re-layouts  3.2 us (1%)
    all_gather x1, waiting for transfers between devices, local(): lax.all_gather(local_grads.astype(jnp.float32), 'dp')  152 us
    all_gather x1, waiting for transfers between devices, local(): lax.all_gather(out_master.astype(jnp.bfloat16), 'dp', axis=0, tiled=True)  22.8 us
    ppermute x5, waiting for transfers between devices, butterfly_sum(): x = x + lax.ppermute(x, axis, [(i, i ^ step) for i in range(size)])  12.5 us
    reduce_sum x1, other arithmetic, local(): jnp.sum(lax.all_gather(local_grads.astype(jnp.float32), 'dp'), axis=0)  7.15 us
  transfers between devices with their start and end apart: 7, of which 7 were waited for; matrix products, arithmetic and copies ran while one was open for 3% of the time, Pallas kernels for 0%

profile of v1, /device:TPU:0, one launch (start us, length us, event | category | flops | bytes accessed | tf_op | source)
XLA Modules:
  0.0 229.6 jit_solution(7802320504929818763)
XLA Ops:
  7.2 2.8 %convert_element_type.35 = f32[1,8,256,256]{3,2,1,0:T(8,128)} convert(bf16[1,8,256,256]{3,2,1,0:T(8,128)(2,1)} %param.9) | non-fusion elementwise | flops 524288 | bytes 3145728 | tf_op jit(solution)/shard_map/convert_element_type | solution.py:54
  10.1 0.1 iota_compare_fusion.1
  10.2 0.2 select_reduce_fusion
  10.4 0.1 fusion.34
  10.6 0.2 dynamic-slice_reduce_fusion.1
  10.8 0.2 and_reduce_fusion
  10.9 0.2 dynamic-slice_reduce_fusion
  11.1 0.2 reduce-window.8
  11.3 0.2 fusion.36
  11.5 152.5 %all-gather.3.cloned.1.call-done = f32[8,8,256,256]{3,2,1,0:T(8,128)} async-done(((f32[1,8,256,256]{3,2,1,0:T(8,128)}), f32[8,8,256,256]{3,2,1,0:T(8,128)}) %all-gather.3.cloned.1.call-update) | async-done | bytes 16777232 | tf_op jit(solution)/shard_map/all_gather | solution.py:54
  164.0 7.2 %reduce_sum.85 = f32[8,256,256]{2,1,0:T(8,128)S(1)} reduce(f32[8,8,256,256]{3,2,1,0:T(8,128)} %all-gather.3.cloned.1.call-done, f32[]{:T(128)} %constant.64.clone.1), dimensions={0}, to_apply=%region_4.5 | reduce | flops 3670016 | bytes 18874372 | tf_op jit(solution)/shard_map/reduce_sum | solution.py:54
  171.2 0.6 gather_fusion
  171.8 0.5 fusion.15
  172.3 1.7 multiply_reduce_fusion
  174.0 0.1 multiply_reduce_fusion.3
  174.1 0.3 collective-permute-start
  174.4 0.9 collective-permute-done
  175.4 3.6 %collective-permute-done.1 = f32[2,9]{1,0:T(2,128)S(1)} collective-permute-done((f32[2,9]{1,0:T(2,128)S(1)}, f32[2,9]{1,0:T(2,128)S(1)}, u32[]{:S(2)}, u32[]{:S(2)}) %collective-permute-start.1) | collective-permute-done | bytes 104 | tf_op jit(solution)/shard_map/ppermute | solution.py:18
  178.9 0.7 collective-permute-start.2
  179.7 3.8 %collective-permute-done.2 = f32[2,9]{1,0:T(2,128)S(1)} collective-permute-done((f32[2,9]{1,0:T(2,128)S(1)}, f32[2,9]{1,0:T(2,128)S(1)}, u32[]{:S(2)}, u32[]{:S(2)}) %collective-permute-start.2) | collective-permute-done | bytes 104 | tf_op jit(solution)/shard_map/ppermute | solution.py:18
  183.5 1.5 collective-permute-start.3
  185.0 2.1 collective-permute-done.3
  187.1 1.5 collective-permute-start.4
  188.5 2.1 collective-permute-done.4
  190.6 0.2 multiply_reduce_fusion.1
  190.9 1.0 fusion.43
  191.9 1.7 fusion.5
  193.6 2.0 fusion.2
  195.6 1.0 fusion.8
  196.5 22.8 %all-gather.5.cloned.1.call-done = bf16[16,256,256]{2,1,0:T(8,128)(2,1)} async-done(((bf16[2,256,256]{2,1,0:T(8,128)(2,1)}), bf16[16,256,256]{2,1,0:T(8,128)(2,1)}) %all-gather.5.cloned.1.call-update) | async-done | bytes 2097168 | tf_op jit(solution)/shard_map/all_gather | solution.py:95
  219.4 2.2 gather_fusion.1
  221.6 1.1 broadcast_select_fusion
  (36 shorter events, 0.4 us)
Async XLA Ops:
  7.2 165.1 %copy-start = (bf16[1,1,2,256,256]{4,3,2,1,0:T(8,128)(2,1)S(1)}, bf16[1,1,2,256,256]{4,3,2,1,0:T(8,128)(2,1)}, u32[]{:S(2)}) copy-start(bf16[1,1,2,256,256]{4,3,2,1,0:T(8,128)(2,1)} %param.15) | copy-start | bytes 786436
  7.2 2.9 %copy-start.5 = (s32[8,1]{0,1:T(1,128)S(1)}, s32[8,1]{0,1:T(1,128)}, u32[]{:S(2)}) copy-start(s32[8,1]{0,1:T(1,128)} %param.10) | copy-start | bytes 100
  7.2 3.9 %copy-start.6 = (s32[9]{0:T(128)S(1)}, s32[9]{0:T(128)}, u32[]{:S(2)}) copy-start(s32[9]{0:T(128)} %param.11) | copy-start | bytes 112
  7.2 156.8 %all-gather.3.cloned.1.call-start = ((), (), s32[]{:S(2)}) async-start(), calls=%async_computation | async-start | bytes 18874368 | tf_op jit(solution)/shard_map/all_gather | solution.py:54
  10.1 209.3 %all-gather.5.cloned.1.call-start = ((), (), s32[]{:S(2)}) async-start(), calls=%async_computation.1 | async-start | bytes 2359296 | tf_op jit(solution)/shard_map/all_gather | solution.py:95
  11.5 160.3 %copy-start.1 = (f32[1,1,2,256,256]{4,3,2,1,0:T(8,128)S(1)}, f32[1,1,2,256,256]{4,3,2,1,0:T(8,128)}, u32[]{:S(2)}) copy-start(f32[1,1,2,256,256]{4,3,2,1,0:T(8,128)} %param.16) | copy-start | bytes 1572868
  171.8 19.1 %copy-start.2 = (f32[1,1,2,256,256]{4,3,2,1,0:T(8,128)S(1)}, f32[1,1,2,256,256]{4,3,2,1,0:T(8,128)}, u32[]{:S(2)}) copy-start(f32[1,1,2,256,256]{4,3,2,1,0:T(8,128)} %param.17) | copy-start | bytes 1572868
  172.3 19.6 %copy-start.3 = (f32[1,1,2,256,256]{4,3,2,1,0:T(8,128)S(1)}, f32[1,1,2,256,256]{4,3,2,1,0:T(8,128)}, u32[]{:S(2)}) copy-start(f32[1,1,2,256,256]{4,3,2,1,0:T(8,128)} %param.12) | copy-start | bytes 1572868
  174.0 19.6 %copy-start.4 = (f32[1,1,2,256,256]{4,3,2,1,0:T(8,128)S(1)}, f32[1,1,2,256,256]{4,3,2,1,0:T(8,128)}, u32[]{:S(2)}) copy-start(f32[1,1,2,256,256]{4,3,2,1,0:T(8,128)} %param.13) | copy-start | bytes 1572868
  174.1 1.2 collective-permute-start
  175.3 3.6 %collective-permute-start.1 = (f32[2,9]{1,0:T(2,128)S(1)}, f32[2,9]{1,0:T(2,128)S(1)}, u32[]{:S(2)}, u32[]{:S(2)}) collective-permute-start(f32[2,9]{1,0:T(2,128)S(1)} %fusion.42), channel_id=1, source_target_pairs={{0,8},{4,12},{8,0},{12,4},{16,24},{20,28},{24,16},{28,20},{1,9},{5... | collective-permute-start | bytes 224 | tf_op jit(solution)/shard_map/ppermute | solution.py:18
  178.9 4.5 %collective-permute-start.2 = (f32[2,9]{1,0:T(2,128)S(1)}, f32[2,9]{1,0:T(2,128)S(1)}, u32[]{:S(2)}, u32[]{:S(2)}) collective-permute-start(f32[2,9]{1,0:T(2,128)S(1)} %fusion.49), channel_id=1, source_target_pairs={{0,16},{4,20},{8,24},{12,28},{16,0},{20,4},{24,8},{28,12},{1,17},{... | collective-permute-start | bytes 224 | tf_op jit(solution)/shard_map/ppermute | solution.py:18
  183.5 3.6 %collective-permute-start.3 = (f32[2,9]{1,0:T(2,128)S(1)}, f32[2,9]{1,0:T(2,128)S(1)}, u32[]{:S(2)}, u32[]{:S(2)}) collective-permute-start(f32[2,9]{1,0:T(2,128)S(1)} %add.92), channel_id=1, source_target_pairs={{0,1},{1,0},{2,3},{3,2},{4,5},{5,4},{6,7},{7,6},{8,9},{9,8},{10,11... | collective-permute-start | bytes 224 | tf_op jit(solution)/shard_map/ppermute | solution.py:18
  187.1 3.6 %collective-permute-start.4 = (f32[2,9]{1,0:T(2,128)S(1)}, f32[2,9]{1,0:T(2,128)S(1)}, u32[]{:S(2)}, u32[]{:S(2)}) collective-permute-start(f32[2,9]{1,0:T(2,128)S(1)} %add.93), channel_id=1, source_target_pairs={{0,2},{1,3},{2,0},{3,1},{4,6},{5,7},{6,4},{7,5},{8,10},{9,11},{10,... | collective-permute-start | bytes 224 | tf_op jit(solution)/shard_map/ppermute | solution.py:18
Sparse Core Ops, SparseCore 0:
  10.2 153.7 all-gather.2
  192.0 27.3 all-gather.4
